TPU v7x, 256 devices: a whole 4x4x8 slice. The times are simulated.
256 devices in a mesh: row: 8 (over y, core), col: 16 (over x_lo, z), req: 2 (over x_hi).
Axes of the slice: x: 4 (x_hi: 2, x_lo: 2; x = x_hi * 2 + x_lo), y: 4, z: 8, core: 2. Of those that a mesh axis runs over, the one named last changes fastest.
Arguments:
- tokens: bfloat16 [3072, 4096], P(('req', 'row'), 'col'), may hold values from -6 to 6
- up_weight: bfloat16 [4096, 21504], P('col', 'row'), may hold values from -0.09375 to 0.09375
- down_weight: bfloat16 [21504, 4096], P('row', 'col'), may hold values from -0.0390625 to 0.0390625
- pool_states: float32 [192, 2, 128, 64, 128], P('row', 'req', 'col'), may hold values from -6 to 6
- pool_edges: float32 [192, 2, 128, 64, 3], P('row', 'req', 'col'), may hold values from -6 to 6
- finish_ids: int32 [32], replicated, may hold values from 0 to 191, as said below
- slot_perm: int32 [32], replicated, may hold values from 0 to 31, each once
Outputs:
- layer_out: bfloat16 [3072, 4096], P(('req', 'row'), 'col')
- decode_states: float32 [32, 2, 128, 64, 128], P('req', None, 'col', 'row')
- decode_edges: float32 [32, 2, 128, 64, 3], P('req', None, 'col', 'row')
Inputs may be any that keep to these rules, and one draw needn't show every extreme that they name: `finish_ids`: entries are distinct; of the 24 slots r * 24 to (r + 1) * 24 - 1 of one index r of row, at most 8 are named, and exactly 8 for some index. `slot_perm`: every decode slot is named once.
All inputs are finite; a program needn't handle non-finite values.
Results may differ from a plain program's by a relative error of at most 0.0044.
Values may be sent and summed in bfloat16 or wider, within the bound.
No kernel may reach another device: no remote copies, remote signals or barrier semaphores. Data moves between devices by JAX's collectives and lax.ppermute only.
A program may use at most 128 MiB of HBM per device.

v0:
```python
import jax
import jax.numpy as jnp
import numpy as np
from jax import lax
from jax.sharding import Mesh
from jax.sharding import PartitionSpec as P

MOST = 8
SWAP = [(0, 1), (1, 0)]


def handover(pool_states, pool_edges, finish_ids, slot_perm):
    local = pool_states.shape[0]
    finished = slot_perm.shape[0]
    r = lax.axis_index("row")
    numbers = jnp.arange(finished, dtype=jnp.int32)
    matches = slot_perm[None, :] == numbers[:, None]
    inverse = jnp.sum(jnp.where(matches, numbers[None, :], 0), axis=1)
    row_of = finish_ids // local
    same = row_of[:, None] == row_of[None, :]
    earlier = numbers[None, :] < numbers[:, None]
    rank = jnp.sum(jnp.where(same & earlier, 1, 0), axis=1)
    slots = jnp.arange(MOST, dtype=jnp.int32)
    chosen = (row_of[None, :] == r) & (rank[None, :] == slots[:, None])
    local_slot = jnp.sum(jnp.where(chosen, finish_ids[None, :] - r * local, 0), axis=1)
    picked = jnp.concatenate([pool_states[local_slot], pool_edges[local_slot]], axis=-1)
    arrived = lax.all_to_all(picked, "row", split_axis=3, concat_axis=0, tiled=True)
    source = inverse
    wanted = row_of[source] * MOST + rank[source]
    rows = arrived[wanted]
    both = lax.all_to_all(rows, "req", split_axis=0, concat_axis=1, tiled=True)
    n = pool_states.shape[-1]
    return (both[..., :n], both[..., n:])


def ffn(tokens, up_weight, down_weight):
    i = lax.axis_index("cx")
    block, width = tokens.shape
    half = block // 2
    halves = tokens.reshape(2, half, width)
    mine = lax.dynamic_index_in_dim(halves, i, 0, keepdims=False)
    theirs = lax.dynamic_index_in_dim(halves, 1 - i, 0, keepdims=False)
    recv = lax.ppermute(theirs, "cx", SWAP)
    xa = jnp.concatenate([mine, recv], axis=1)
    xg = lax.all_gather(xa, "row", axis=0, tiled=True)
    w1 = jnp.concatenate([up_weight, lax.ppermute(up_weight, "cx", SWAP)], axis=0)
    preact = lax.psum_scatter(
        jnp.dot(xg, w1, preferred_element_type=jnp.float32), "cz", scatter_dimension=0, tiled=True
    )
    active = jnp.maximum(preact, 0.0)
    hidden = (active * active).astype(jnp.bfloat16)
    hg = lax.all_gather(hidden, "cz", axis=0, tiled=True)
    w2 = jnp.concatenate([down_weight, lax.ppermute(down_weight, "cx", SWAP)], axis=1)
    products = jnp.dot(hg, w2, preferred_element_type=jnp.float32)
    summed = lax.psum_scatter(products, "row", scatter_dimension=0, tiled=True)
    own = summed[:, :width]
    other = lax.ppermute(summed[:, width:], "cx", SWAP)
    full = jnp.where(i == 0, jnp.concatenate([own, other], 0), jnp.concatenate([other, own], 0))
    return (tokens.astype(jnp.float32) + full).astype(jnp.bfloat16)


def on_device(tokens, up_weight, down_weight, pool_states, pool_edges, finish_ids, slot_perm):
    layer_out = ffn(tokens, up_weight, down_weight)
    decode_states, decode_edges = handover(pool_states, pool_edges, finish_ids, slot_perm)
    return (layer_out, decode_states, decode_edges)


def solution(mesh):
    devices = np.asarray(mesh.devices)
    rows, cols, reqs = devices.shape
    split = Mesh(devices.reshape(rows, 2, cols // 2, reqs), ("row", "cx", "cz", "req"))
    col = ("cx", "cz")
    in_specs = (
        P(("req", "row"), col),
        P(col, "row"),
        P("row", col),
        P("row", "req", col, None, None),
        P("row", "req", col, None, None),
        P(),
        P(),
    )
    out_specs = (
        P(("req", "row"), col),
        P("req", None, col, "row", None),
        P("req", None, col, "row", None),
    )
    return jax.shard_map(
        on_device, mesh=split, in_specs=in_specs, out_specs=out_specs, check_vma=False
    )
```

profile of v0, /device:TPU:2, one launch (start us, length us, event | category | flops | bytes accessed | tf_op | source)
XLA Modules:
  0.0 343.2 jit_solution(12249648840841902804)
XLA Ops:
  7.2 2.3 collective-permute-start.1
  10.5 30.0 %collective-permute-done = bf16[96,256]{1,0:T(8,128)(2,1)S(1)} collective-permute-done((bf16[96,256]{1,0:T(8,128)(2,1)S(1)}, bf16[96,256]{1,0:T(8,128)(2,1)S(1)}, u32[]{:S(2)}, u32[]{:S(2)}) %collective-permute-start) | collective-permute-done | bytes 49184 | tf_op jit(solution)/shard_map/ppermute | solution.py:43
  40.5 13.9 %all_gather.6 = bf16[768,512]{1,0:T(8,128)(2,1)S(1)} all-gather(bf16[96,512]{1,0:T(8,128)(2,1)S(1)} %pad_maximum_fusion.1), channel_id=1, replica_groups=mesh['row'=8,'cx'=2,'cz'=8,'req'=2] {'row'}, dimensions={0}, use_global_device_ids=true | all-gather | bytes 884736 | tf_op jit(solution)/shard_map/all_gather | solution.py:45
  54.4 6.9 %fusion = f32[768,2688]{1,0:T(8,128)} fusion(bf16[768,512]{1,0:T(8,128)(2,1)S(1)} %all_gather.6, bf16[256,2688]{1,0:T(8,128)(2,1)S(1)} %collective-permute-done.1, bf16[256,2688]{1,0:T(8,128)(2,1)} %param.8), kind=kOutput, calls=%fused_computation.7 | convolution fusion | flops 2119434240 | bytes 11796480 | tf_op jit(solution)/shard_map/dot_general | solution.py:48
  61.4 96.0 %reduce-scatter.3.cloned.1.call-done = f32[96,2688]{1,0:T(8,128)} async-done(((f32[768,2688]{1,0:T(8,128)}), f32[96,2688]{1,0:T(8,128)}) %reduce-scatter.3.cloned.1.call-update) | async-done | bytes 1032208 | tf_op jit(solution)/shard_map/reduce_scatter | solution.py:47
  157.5 2.1 multiply_convert_fusion
  160.3 31.3 %collective-permute-done.2 = bf16[2688,256]{1,0:T(8,128)(2,1)S(1)} collective-permute-done((bf16[2688,256]{1,0:T(8,128)(2,1)S(1)}, bf16[2688,256]{1,0:T(8,128)(2,1)S(1)}, u32[]{:S(2)}, u32[]{:S(2)}) %collective-permute-start.2) | collective-permute-done | bytes 1376288 | tf_op jit(solution)/shard_map/ppermute | solution.py:53
  191.6 21.0 %all-gather.2.cloned.1.call-done = bf16[768,2688]{1,0:T(8,128)(2,1)} async-done(((bf16[96,2688]{1,0:T(8,128)(2,1)}), bf16[768,2688]{1,0:T(8,128)(2,1)}) %all-gather.2.cloned.1.call-update) | async-done | bytes 4128784 | tf_op jit(solution)/shard_map/all_gather | solution.py:52
  212.7 5.7 %fusion.4 = f32[768,512]{1,0:T(8,128)} fusion(bf16[768,2688]{1,0:T(8,128)(2,1)} %all-gather.2.cloned.1.call-done, bf16[2688,256]{1,0:T(8,128)(2,1)S(1)} %collective-permute-done.2, bf16[2688,256]{1,0:T(8,128)(2,1)S(1)} %copy-done.4), kind=kOutput, calls=%fused_computation.11 | convolution fusion | flops 2119434240 | bytes 8454144 | tf_op jit(solution)/shard_map/dot_general | solution.py:54
  220.1 4.8 %gather_fusion = f32[8,8,64,128]{3,2,1,0:T(8,128)} fusion(f32[24,8,64,128]{3,2,1,0:T(8,128)} %bitcast.45, s32[1024]{0:T(1024)S(1)} %pad_clamp_fusion.2), kind=kCustom, calls=%fused_computation | custom fusion | bytes 4194336 | tf_op jit(solution)/shard_map/gather | solution.py:26
  224.9 2.0 pad_maximum_fusion
  226.9 4.4 %copy.36 = f32[8,1,8,64,131]{4,2,0,1,3:T(8,128)} copy(f32[8,1,8,64,131]{4,3,2,0,1:T(8,128)S(1)} %pad_maximum_fusion) | data formatting | bytes 4292608 | tf_op jit(solution)/shard_map/concatenate | solution.py:26
  231.3 4.9 %all-to-all-start = ((f32[8,1,8,64,131]{4,2,0,1,3:T(8,128)}), f32[8,1,8,64,131]{4,2,0,1,3:T(8,128)}, u32[]{:S(2)}, u32[]{:S(2)}) async-start(f32[8,1,8,64,131]{4,2,0,1,3:T(8,128)} %copy.36), calls=%async_computation.2 | async-start | bytes 8388608 | tf_op jit(solution)/shard_map/all_to_all | solution.py:27
  237.8 51.6 %all-to-all-done = f32[8,1,8,64,131]{4,2,0,1,3:T(8,128)} async-done(((f32[8,1,8,64,131]{4,2,0,1,3:T(8,128)}), f32[8,1,8,64,131]{4,2,0,1,3:T(8,128)}, u32[]{:S(2)}, u32[]{:S(2)}) %all-to-all-start) | async-done | bytes 2146336 | tf_op jit(solution)/shard_map/all_to_all | solution.py:27
  289.4 4.6 %copy.43 = f32[8,1,8,64,131]{4,3,2,0,1:T(8,128)S(1)} copy(f32[8,1,8,64,131]{4,2,0,1,3:T(8,128)} %all-to-all-done) | data formatting | bytes 4292608 | tf_op jit(solution)/shard_map/all_to_all | solution.py:27
  294.0 2.6 copy.38
  296.6 4.2 %gather_fusion.4 = f32[32,8,8,131]{3,2,1,0:T(8,128)} fusion(f32[64,8,8,131]{3,2,1,0:T(8,128)} %bitcast.39, s32[1024]{0:T(1024)S(1)} %pad_clamp_fusion), kind=kCustom, calls=%fused_computation.4 | custom fusion | bytes 2146432 | tf_op jit(solution)/shard_map/gather | solution.py:30
  300.7 3.8 %all-to-all-start.1 = ((f32[32,1,8,8,131]{4,3,2,1,0:T(8,128)}), f32[32,1,8,8,131]{4,3,2,1,0:T(8,128)S(1)}, u32[]{:S(2)}, u32[]{:S(2)}) async-start(f32[32,1,8,8,131]{4,3,2,1,0:T(8,128)} %bitcast.42), calls=%async_computation.3 | async-start | bytes 4194304 | tf_op jit(solution)/shard_map/all_to_all | solution.py:31
  304.5 1.6 fusion.17
  306.2 1.0 collective-permute-start.3
  307.2 25.0 %all-to-all-done.1 = f32[32,1,8,8,131]{4,3,2,1,0:T(8,128)S(1)} async-done(((f32[32,1,8,8,131]{4,3,2,1,0:T(8,128)}), f32[32,1,8,8,131]{4,3,2,1,0:T(8,128)S(1)}, u32[]{:S(2)}, u32[]{:S(2)}) %all-to-all-start.1) | async-done | bytes 1073184 | tf_op jit(solution)/shard_map/all_to_all | solution.py:31
  332.3 1.1 copy.40
  333.4 1.5 copy.41
  335.0 1.6 fusion.9
  (42 shorter events, 5.1 us)
Async XLA Ops:
  7.2 211.6 %copy-start = (f32[24,1,8,64,3]{3,2,4,1,0:T(8,128)S(1)}, f32[24,1,8,64,3]{3,2,4,1,0:T(8,128)}, u32[]{:S(2)}) copy-start(f32[24,1,8,64,3]{3,2,4,1,0:T(8,128)} %param.11) | copy-start | bytes 442372
  7.2 150.3 %reduce-scatter.3.cloned.1.call-start = ((), (), s32[]{:S(2)}) async-start(), calls=%async_computation.4 | async-start | bytes 9289728 | tf_op jit(solution)/shard_map/reduce_scatter | solution.py:47
  7.2 47.2 %collective-permute-start.1 = (bf16[256,2688]{1,0:T(8,128)(2,1)}, bf16[256,2688]{1,0:T(8,128)(2,1)S(1)}, u32[]{:S(2)}, u32[]{:S(2)}) collective-permute-start(bf16[256,2688]{1,0:T(8,128)(2,1)} %param.8), channel_id=1, source_target_pairs={{0,16},{16,0},{1,17},{17,1},{2,18},{18,2},{3,19},{19,3},{4,20},{20... | collective-permute-start | bytes 4128776 | tf_op jit(solution)/shard_map/ppermute | solution.py:46
  10.4 30.1 %collective-permute-start = (bf16[96,256]{1,0:T(8,128)(2,1)S(1)}, bf16[96,256]{1,0:T(8,128)(2,1)S(1)}, u32[]{:S(2)}, u32[]{:S(2)}) collective-permute-start(bf16[96,256]{1,0:T(8,128)(2,1)S(1)} %get-tuple-element.29), channel_id=1, source_target_pairs={{0,16},{16,0},{1,17},{17,1},{2,18},{18,2},{3,19},{19,3},{4,20},{20... | collective-permute-start | bytes 147464 | tf_op jit(solution)/shard_map/ppermute | solution.py:43
  61.4 98.3 %copy-start.4 = (bf16[2688,256]{1,0:T(8,128)(2,1)S(1)}, bf16[2688,256]{1,0:T(8,128)(2,1)}, u32[]{:S(2)}) copy-start(bf16[2688,256]{1,0:T(8,128)(2,1)} %param.9) | copy-start | bytes 4128772
  61.4 151.3 %all-gather.2.cloned.1.call-start = ((), (), s32[]{:S(2)}) async-start(), calls=%async_computation.5 | async-start | bytes 4644864 | tf_op jit(solution)/shard_map/all_gather | solution.py:52
  159.6 144.9 %reduce-scatter.5.cloned.1.call-start = ((), (), s32[]{:S(2)}) async-start(), calls=%async_computation.6 | async-start | bytes 1769472 | tf_op jit(solution)/shard_map/reduce_scatter | solution.py:55
  159.6 32.0 %collective-permute-start.2 = (bf16[2688,256]{1,0:T(8,128)(2,1)S(1)}, bf16[2688,256]{1,0:T(8,128)(2,1)S(1)}, u32[]{:S(2)}, u32[]{:S(2)}) collective-permute-start(bf16[2688,256]{1,0:T(8,128)(2,1)S(1)} %copy-done.4), channel_id=1, source_target_pairs={{0,16},{16,0},{1,17},{17,1},{2,18},{18,2},{3,19},{19,3},{4,20},{20... | collective-permute-start | bytes 4128776 | tf_op jit(solution)/shard_map/ppermute | solution.py:53
  160.3 58.1 %copy-start.3 = (s32[32]{0:T(128)S(1)}, s32[32]{0:T(128)}, u32[]{:S(2)}) copy-start(s32[32]{0:T(128)} %param.12) | copy-start | bytes 388
  231.3 4.9 %copy-start.5 = (s32[32]{0:T(128)S(1)}, s32[32]{0:T(128)}, u32[]{:S(2)}) copy-start(s32[32]{0:T(128)} %param.13) | copy-start | bytes 388
  231.3 58.0 %all-to-all-start = ((f32[8,1,8,64,131]{4,2,0,1,3:T(8,128)}), f32[8,1,8,64,131]{4,2,0,1,3:T(8,128)}, u32[]{:S(2)}, u32[]{:S(2)}) async-start(f32[8,1,8,64,131]{4,2,0,1,3:T(8,128)} %copy.36), calls=%async_computation.2 | async-start | bytes 8388608 | tf_op jit(solution)/shard_map/all_to_all | solution.py:27
  300.7 31.4 %all-to-all-start.1 = ((f32[32,1,8,8,131]{4,3,2,1,0:T(8,128)}), f32[32,1,8,8,131]{4,3,2,1,0:T(8,128)S(1)}, u32[]{:S(2)}, u32[]{:S(2)}) async-start(f32[32,1,8,8,131]{4,3,2,1,0:T(8,128)} %bitcast.42), calls=%async_computation.3 | async-start | bytes 4194304 | tf_op jit(solution)/shard_map/all_to_all | solution.py:31
  306.2 28.8 %collective-permute-start.3 = (f32[96,256]{1,0:T(8,128)}, f32[96,256]{1,0:T(8,128)}, u32[]{:S(2)}, u32[]{:S(2)}) collective-permute-start(f32[96,256]{1,0:T(8,128)} %get-tuple-element.27), channel_id=1, source_target_pairs={{0,16},{16,0},{1,17},{17,1},{2,18},{18,2},{3,19},{19,3},{4,20},{20... | collective-permute-start | bytes 294920 | tf_op jit(solution)/shard_map/ppermute | solution.py:57
  332.2 2.8 copy-start.1
  332.3 2.7 copy-start.2
Sparse Core Ops, SparseCore 0:
  61.5 95.9 reduce-scatter.2
  159.8 52.7 all-gather.1
  218.5 41.6 reduce-scatter.4
where the time goes:
time: 344 us; the launch traced here: 343 us
  waiting for transfers between devices  255 us (74%)
  local copies, waits for them, and re-layouts  28.5 us (8%)
  blocking collectives  13.9 us (4%)
  between operations  13.9 us (4%)
  starting transfers between devices  12.8 us (4%)
  matrix products  12.7 us (4%)
  other arithmetic  6.26 us (2%)
    reduce_scatter x1, waiting for transfers between devices, ffn(): lax.psum_scatter(jnp.dot(xg, w1, preferred_element_type=jnp.float32), 'cz...  96 us
    all_to_all x1, waiting for transfers between devices, handover(): lax.all_to_all(picked, 'row', split_axis=3, concat_axis=0, tiled=True)  51.6 us
    ppermute x1, waiting for transfers between devices, ffn(): lax.ppermute(down_weight, 'cx', SWAP)  31.3 us
    ppermute x1, waiting for transfers between devices, ffn(): recv = lax.ppermute(theirs, 'cx', SWAP)  30 us
    all_to_all x1, waiting for transfers between devices, handover(): both = lax.all_to_all(rows, 'req', split_axis=0, concat_axis=1, tiled=True)  25 us
    all_gather x1, waiting for transfers between devices, ffn(): hg = lax.all_gather(hidden, 'cz', axis=0, tiled=True)  21 us
    all_gather x1, blocking collectives, ffn(): xg = lax.all_gather(xa, 'row', axis=0, tiled=True)  13.9 us
    all_to_all x2, local copies, waits for them, and re-layouts, handover(): lax.all_to_all(picked, 'row', split_axis=3, concat_axis=0, tiled=True)  7.19 us
  transfers between devices with their start and end apart: 9, of which 6 were waited for; matrix products, arithmetic and copies ran while one was open for 9% of the time, Pallas kernels for 0%

commit v1 on v0

--- a/solution.py
+++ b/solution.py
@@ -1,3 +1,4 @@
+import functools
 import jax
 import jax.numpy as jnp
 import numpy as np
@@ -7,6 +8,19 @@
 
 MOST = 8
 SWAP = [(0, 1), (1, 0)]
+
+
+def advance_waves_by_axis(field, lane_axis):
+    before = lax.all_to_all(
+        jnp.stack(tuple((field for _ in range(lax.axis_size(lane_axis))))),
+        lane_axis,
+        split_axis=0,
+        concat_axis=0,
+    )
+    return jnp.concatenate(before, axis=0)
+
+
+time_the_object = functools.partial(advance_waves_by_axis, lane_axis="cz")
 
 
 def handover(pool_states, pool_edges, finish_ids, slot_perm):
@@ -49,7 +63,7 @@
     )
     active = jnp.maximum(preact, 0.0)
     hidden = (active * active).astype(jnp.bfloat16)
-    hg = lax.all_gather(hidden, "cz", axis=0, tiled=True)
+    hg = time_the_object(hidden)
     w2 = jnp.concatenate([down_weight, lax.ppermute(down_weight, "cx", SWAP)], axis=1)
     products = jnp.dot(hg, w2, preferred_element_type=jnp.float32)
     summed = lax.psum_scatter(products, "row", scatter_dimension=0, tiled=True)

time: 344 us -> 391 us (1.14)
  waiting for transfers between devices: 255 us -> 296 us
  starting transfers between devices: 12.8 us -> 17.5 us
    all_to_all x0 -> x1, waiting for transfers between devices: none -> 63 us  [advance_waves_by_axis(): lax.all_to_all(jnp.stack(tuple((field for _ in range(lax.axis_size(lane_a...]
    all_gather x1 -> x0, waiting for transfers between devices: 21 us -> none  [ffn(): hg = lax.all_gather(hidden, 'cz', axis=0, tiled=True)]
    all_to_all x0 -> x1, starting transfers between devices: none -> 4.67 us  [advance_waves_by_axis(): lax.all_to_all(jnp.stack(tuple((field for _ in range(lax.axis_size(lane_a...]
  transfers between devices with their start and end apart: 9 -> 9, of which waited for: 6 -> 6; matrix products, arithmetic and copies ran while one was open for 9% -> 8% of each run, Pallas kernels for 0% -> 0%
where the time goes in v1:
time: 391 us
  waiting for transfers between devices  296 us (76%)
  local copies, waits for them, and re-layouts  30.8 us (8%)
  starting transfers between devices  17.5 us (4%)
  between operations  14.2 us (4%)
  blocking collectives  13.9 us (4%)
  matrix products  12.7 us (3%)
  other arithmetic  5.58 us (1%)
    reduce_scatter x1, waiting for transfers between devices, ffn(): lax.psum_scatter(jnp.dot(xg, w1, preferred_element_type=jnp.float32), 'cz...  96.1 us
    all_to_all x1, waiting for transfers between devices, advance_waves_by_axis(): lax.all_to_all(jnp.stack(tuple((field for _ in range(lax.axis_size(lane_a...  63 us
    all_to_all x1, waiting for transfers between devices, handover(): lax.all_to_all(picked, 'row', split_axis=3, concat_axis=0, tiled=True)  50.8 us
    ppermute x1, waiting for transfers between devices, ffn(): lax.ppermute(down_weight, 'cx', SWAP)  31.3 us
    ppermute x1, waiting for transfers between devices, ffn(): recv = lax.ppermute(theirs, 'cx', SWAP)  30 us
    all_to_all x1, waiting for transfers between devices, handover(): both = lax.all_to_all(rows, 'req', split_axis=0, concat_axis=1, tiled=True)  24.8 us
    all_gather x1, blocking collectives, ffn(): xg = lax.all_gather(xa, 'row', axis=0, tiled=True)  13.9 us
  transfers between devices with their start and end apart: 9, of which 6 were waited for; matrix products, arithmetic and copies ran while one was open for 8% of the time, Pallas kernels for 0%

profile of v1, /device:TPU:2, one launch (start us, length us, event | category | flops | bytes accessed | tf_op | source)
XLA Modules:
  0.0 390.7 jit_solution(1998561989503055132)
XLA Ops:
  7.2 2.3 collective-permute-start.1
  10.5 30.0 %collective-permute-done = bf16[96,256]{1,0:T(8,128)(2,1)S(1)} collective-permute-done((bf16[96,256]{1,0:T(8,128)(2,1)S(1)}, bf16[96,256]{1,0:T(8,128)(2,1)S(1)}, u32[]{:S(2)}, u32[]{:S(2)}) %collective-permute-start) | collective-permute-done | bytes 49184 | tf_op jit(solution)/shard_map/ppermute | solution.py:57
  40.5 13.9 %all_gather.3 = bf16[768,512]{1,0:T(8,128)(2,1)S(1)} all-gather(bf16[96,512]{1,0:T(8,128)(2,1)S(1)} %pad_maximum_fusion.1), channel_id=1, replica_groups=mesh['row'=8,'cx'=2,'cz'=8,'req'=2] {'row'}, dimensions={0}, use_global_device_ids=true | all-gather | bytes 884736 | tf_op jit(solution)/shard_map/all_gather | solution.py:59
  54.4 6.9 %fusion = f32[768,2688]{1,0:T(8,128)} fusion(bf16[768,512]{1,0:T(8,128)(2,1)S(1)} %all_gather.3, bf16[256,2688]{1,0:T(8,128)(2,1)S(1)} %collective-permute-done.1, bf16[256,2688]{1,0:T(8,128)(2,1)} %param.8), kind=kOutput, calls=%fused_computation.7 | convolution fusion | flops 2119434240 | bytes 11796480 | tf_op jit(solution)/shard_map/dot_general | solution.py:62
  61.4 96.1 %reduce-scatter.3.cloned.1.call-done = f32[96,2688]{1,0:T(8,128)} async-done(((f32[768,2688]{1,0:T(8,128)}), f32[96,2688]{1,0:T(8,128)}) %reduce-scatter.3.cloned.1.call-update) | async-done | bytes 1032208 | tf_op jit(solution)/shard_map/reduce_scatter | solution.py:61
  157.5 1.3 multiply_convert_fusion
  158.8 2.2 stack.2
  161.0 4.7 %all-to-all-start = ((bf16[8,96,2688]{2,1,0:T(8,128)(2,1)}), bf16[8,96,2688]{2,1,0:T(8,128)(2,1)}, u32[]{:S(2)}, u32[]{:S(2)}) async-start(bf16[8,96,2688]{2,1,0:T(8,128)(2,1)} %stack.2), calls=%async_computation.1 | async-start | bytes 8257536 | tf_op jit(solution)/shard_map/all_to_all | solution.py:14
  166.4 31.3 %collective-permute-done.2 = bf16[2688,256]{1,0:T(8,128)(2,1)S(1)} collective-permute-done((bf16[2688,256]{1,0:T(8,128)(2,1)S(1)}, bf16[2688,256]{1,0:T(8,128)(2,1)S(1)}, u32[]{:S(2)}, u32[]{:S(2)}) %collective-permute-start.2) | collective-permute-done | bytes 1376288 | tf_op jit(solution)/shard_map/ppermute | solution.py:67
  197.7 63.0 %all-to-all-done = bf16[8,96,2688]{2,1,0:T(8,128)(2,1)} async-done(((bf16[8,96,2688]{2,1,0:T(8,128)(2,1)}), bf16[8,96,2688]{2,1,0:T(8,128)(2,1)}, u32[]{:S(2)}, u32[]{:S(2)}) %all-to-all-start) | async-done | bytes 4128800 | tf_op jit(solution)/shard_map/all_to_all | solution.py:14
  260.8 5.8 %fusion.4 = f32[768,512]{1,0:T(8,128)} fusion(bf16[768,2688]{1,0:T(8,128)(2,1)} %bitcast.3, bf16[2688,256]{1,0:T(8,128)(2,1)S(1)} %collective-permute-done.2, bf16[2688,256]{1,0:T(8,128)(2,1)S(1)} %copy-done.4), kind=kOutput, calls=%fused_computation.11 | convolution fusion | flops 2119434240 | bytes 8454144 | tf_op jit(solution)/shard_map/dot_general | solution.py:68
  268.2 4.8 %gather_fusion = f32[8,8,64,128]{3,2,1,0:T(8,128)} fusion(f32[24,8,64,128]{3,2,1,0:T(8,128)} %bitcast.46, s32[1024]{0:T(1024)S(1)} %pad_clamp_fusion.2), kind=kCustom, calls=%fused_computation | custom fusion | bytes 4194336 | tf_op jit(solution)/shard_map/gather | solution.py:40
  273.0 2.2 pad_maximum_fusion
  275.2 4.4 %copy.36 = f32[8,1,8,64,131]{4,2,0,1,3:T(8,128)} copy(f32[8,1,8,64,131]{4,3,2,0,1:T(8,128)S(1)} %pad_maximum_fusion) | data formatting | bytes 4292608 | tf_op jit(solution)/shard_map/concatenate | solution.py:40
  279.6 4.9 %all-to-all-start.1 = ((f32[8,1,8,64,131]{4,2,0,1,3:T(8,128)}), f32[8,1,8,64,131]{4,2,0,1,3:T(8,128)}, u32[]{:S(2)}, u32[]{:S(2)}) async-start(f32[8,1,8,64,131]{4,2,0,1,3:T(8,128)} %copy.36), calls=%async_computation.3 | async-start | bytes 8388608 | tf_op jit(solution)/shard_map/all_to_all | solution.py:41
  286.0 50.8 %all-to-all-done.1 = f32[8,1,8,64,131]{4,2,0,1,3:T(8,128)} async-done(((f32[8,1,8,64,131]{4,2,0,1,3:T(8,128)}), f32[8,1,8,64,131]{4,2,0,1,3:T(8,128)}, u32[]{:S(2)}, u32[]{:S(2)}) %all-to-all-start.1) | async-done | bytes 2146336 | tf_op jit(solution)/shard_map/all_to_all | solution.py:41
  336.8 4.6 %copy.43 = f32[8,1,8,64,131]{4,3,2,0,1:T(8,128)S(1)} copy(f32[8,1,8,64,131]{4,2,0,1,3:T(8,128)} %all-to-all-done.1) | data formatting | bytes 4292608 | tf_op jit(solution)/shard_map/all_to_all | solution.py:41
  341.4 2.6 copy.38
  344.0 4.2 %gather_fusion.4 = f32[32,8,8,131]{3,2,1,0:T(8,128)} fusion(f32[64,8,8,131]{3,2,1,0:T(8,128)} %bitcast.40, s32[1024]{0:T(1024)S(1)} %pad_clamp_fusion), kind=kCustom, calls=%fused_computation.4 | custom fusion | bytes 2146432 | tf_op jit(solution)/shard_map/gather | solution.py:44
  348.2 3.8 all-to-all-start.2
  352.0 1.6 fusion.17
  354.6 24.8 %all-to-all-done.2 = f32[32,1,8,8,131]{4,3,2,1,0:T(8,128)S(1)} async-done(((f32[32,1,8,8,131]{4,3,2,1,0:T(8,128)}), f32[32,1,8,8,131]{4,3,2,1,0:T(8,128)S(1)}, u32[]{:S(2)}, u32[]{:S(2)}) %all-to-all-start.2) | async-done | bytes 1073184 | tf_op jit(solution)/shard_map/all_to_all | solution.py:45
  380.7 1.5 copy.41
  382.2 1.6 fusion.9
  (42 shorter events, 7.1 us)
Async XLA Ops:
  7.2 259.7 %copy-start = (f32[24,1,8,64,3]{3,2,4,1,0:T(8,128)S(1)}, f32[24,1,8,64,3]{3,2,4,1,0:T(8,128)}, u32[]{:S(2)}) copy-start(f32[24,1,8,64,3]{3,2,4,1,0:T(8,128)} %param.11) | copy-start | bytes 442372
  7.2 150.3 %reduce-scatter.3.cloned.1.call-start = ((), (), s32[]{:S(2)}) async-start(), calls=%async_computation.5 | async-start | bytes 9289728 | tf_op jit(solution)/shard_map/reduce_scatter | solution.py:61
  7.2 47.2 %collective-permute-start.1 = (bf16[256,2688]{1,0:T(8,128)(2,1)}, bf16[256,2688]{1,0:T(8,128)(2,1)S(1)}, u32[]{:S(2)}, u32[]{:S(2)}) collective-permute-start(bf16[256,2688]{1,0:T(8,128)(2,1)} %param.8), channel_id=1, source_target_pairs={{0,16},{16,0},{1,17},{17,1},{2,18},{18,2},{3,19},{19,3},{4,20},{20... | collective-permute-start | bytes 4128776 | tf_op jit(solution)/shard_map/ppermute | solution.py:60
  10.4 30.1 %collective-permute-start = (bf16[96,256]{1,0:T(8,128)(2,1)S(1)}, bf16[96,256]{1,0:T(8,128)(2,1)S(1)}, u32[]{:S(2)}, u32[]{:S(2)}) collective-permute-start(bf16[96,256]{1,0:T(8,128)(2,1)S(1)} %get-tuple-element.29), channel_id=1, source_target_pairs={{0,16},{16,0},{1,17},{17,1},{2,18},{18,2},{3,19},{19,3},{4,20},{20... | collective-permute-start | bytes 147464 | tf_op jit(solution)/shard_map/ppermute | solution.py:57
  161.0 4.7 %copy-start.4 = (bf16[2688,256]{1,0:T(8,128)(2,1)S(1)}, bf16[2688,256]{1,0:T(8,128)(2,1)}, u32[]{:S(2)}) copy-start(bf16[2688,256]{1,0:T(8,128)(2,1)} %param.9) | copy-start | bytes 4128772
  161.0 99.7 %all-to-all-start = ((bf16[8,96,2688]{2,1,0:T(8,128)(2,1)}), bf16[8,96,2688]{2,1,0:T(8,128)(2,1)}, u32[]{:S(2)}, u32[]{:S(2)}) async-start(bf16[8,96,2688]{2,1,0:T(8,128)(2,1)} %stack.2), calls=%async_computation.1 | async-start | bytes 8257536 | tf_op jit(solution)/shard_map/all_to_all | solution.py:14
  165.7 186.3 %reduce-scatter.5.cloned.1.call-start = ((), (), s32[]{:S(2)}) async-start(), calls=%async_computation.6 | async-start | bytes 1769472 | tf_op jit(solution)/shard_map/reduce_scatter | solution.py:69
  165.8 32.0 %collective-permute-start.2 = (bf16[2688,256]{1,0:T(8,128)(2,1)S(1)}, bf16[2688,256]{1,0:T(8,128)(2,1)S(1)}, u32[]{:S(2)}, u32[]{:S(2)}) collective-permute-start(bf16[2688,256]{1,0:T(8,128)(2,1)S(1)} %copy-done.4), channel_id=1, source_target_pairs={{0,16},{16,0},{1,17},{17,1},{2,18},{18,2},{3,19},{19,3},{4,20},{20... | collective-permute-start | bytes 4128776 | tf_op jit(solution)/shard_map/ppermute | solution.py:67
  260.8 5.8 %copy-start.3 = (s32[32]{0:T(128)S(1)}, s32[32]{0:T(128)}, u32[]{:S(2)}) copy-start(s32[32]{0:T(128)} %param.12) | copy-start | bytes 388
  279.6 4.9 %copy-start.5 = (s32[32]{0:T(128)S(1)}, s32[32]{0:T(128)}, u32[]{:S(2)}) copy-start(s32[32]{0:T(128)} %param.13) | copy-start | bytes 388
  279.6 57.2 %all-to-all-start.1 = ((f32[8,1,8,64,131]{4,2,0,1,3:T(8,128)}), f32[8,1,8,64,131]{4,2,0,1,3:T(8,128)}, u32[]{:S(2)}, u32[]{:S(2)}) async-start(f32[8,1,8,64,131]{4,2,0,1,3:T(8,128)} %copy.36), calls=%async_computation.3 | async-start | bytes 8388608 | tf_op jit(solution)/shard_map/all_to_all | solution.py:41
  348.2 31.2 %all-to-all-start.2 = ((f32[32,1,8,8,131]{4,3,2,1,0:T(8,128)}), f32[32,1,8,8,131]{4,3,2,1,0:T(8,128)S(1)}, u32[]{:S(2)}, u32[]{:S(2)}) async-start(f32[32,1,8,8,131]{4,3,2,1,0:T(8,128)} %bitcast.43), calls=%async_computation.4 | async-start | bytes 4194304 | tf_op jit(solution)/shard_map/all_to_all | solution.py:45
  353.6 28.6 %collective-permute-start.3 = (f32[96,256]{1,0:T(8,128)}, f32[96,256]{1,0:T(8,128)}, u32[]{:S(2)}, u32[]{:S(2)}) collective-permute-start(f32[96,256]{1,0:T(8,128)} %get-tuple-element.27), channel_id=1, source_target_pairs={{0,16},{16,0},{1,17},{17,1},{2,18},{18,2},{3,19},{19,3},{4,20},{20... | collective-permute-start | bytes 294920 | tf_op jit(solution)/shard_map/ppermute | solution.py:71
  379.5 2.8 copy-start.1
  379.6 2.7 copy-start.2
Sparse Core Ops, SparseCore 0:
  61.5 95.9 reduce-scatter.2
  266.7 39.3 reduce-scatter.4
